TPU v7x, 32 devices: a whole 2x2x4 slice. The times are simulated.
32 devices in a mesh: dp: 8 (over z, y), feat: 4 (over x, core).
Axes of the slice: x: 2, y: 2, z: 4, core: 2. Of those that a mesh axis runs over, the one named last changes fastest.
Arguments:
- activations: bfloat16 [16384, 2048], P('feat', 'dp'), may hold values from -6 to 6
- cotangent: bfloat16 [16384, 2048], P('feat', 'dp'), may hold values from -6 to 6
- r_mix: bfloat16 [64, 256, 256], P('feat', 'dp'), may hold values from -0.375 to 0.375
- l_mix: bfloat16 [256, 4096], P('feat', 'dp'), may hold values from -0.75 to 0.75
Outputs:
- grad_x: bfloat16 [16384, 2048], P('feat', 'dp')
- grad_r: float32 [64, 256, 256], P('feat', 'dp')
- grad_l: float32 [256, 4096], P('feat', 'dp')
All inputs are finite; a program needn't handle non-finite values.
Results may differ from a plain program's by a relative error of at most 0.0055.
Values may be sent and summed in bfloat16 or wider, within the bound.
No kernel may reach another device: no remote copies, remote signals or barrier semaphores. Data moves between devices by JAX's collectives and lax.ppermute only.
A program may use at most 64 MiB of HBM per device.

v0:
```python
import math
import jax
import jax.numpy as jnp
from jax import lax
from jax.sharding import PartitionSpec as P

BLOCKS = 64
WIDTH = 256


def gelu_tanh(values):
    return jax.nn.gelu(values, approximate=True)


def slope_of(pre_act, upstream):
    _, pullback = jax.vjp(gelu_tanh, pre_act)
    return pullback(upstream.astype(jnp.float32))[0].astype(jnp.bfloat16)


def body(activations, cotangent, r_mix, l_mix):
    tok_count = activations.shape[1]
    local_blocks = activations.shape[0] // WIDTH
    grad_scale = 1.0 / math.sqrt(tok_count * lax.axis_size("dp"))
    r_whole, l_whole = (
        lax.all_gather(r_mix, "dp", axis=1, tiled=True),
        lax.all_gather(l_mix, "dp", axis=1, tiled=True),
    )
    local_cols = l_whole.shape[0]
    l_blocks = l_whole.reshape(local_cols, BLOCKS, BLOCKS)
    x_blocks = activations.reshape(local_blocks, WIDTH, tok_count)
    g_blocks = cotangent.reshape(local_blocks, WIDTH, tok_count)
    mixed_rows = jnp.einsum(
        "bit,bio->bot", x_blocks, r_whole, preferred_element_type=jnp.float32
    ).astype(jnp.bfloat16)
    outgoing = (mixed_rows,)
    parts = (lax.all_to_all(outgoing[0], "feat", split_axis=1, concat_axis=0, tiled=True),)
    columns = parts[0]
    pre_act = jnp.einsum("bst,sbc->cst", columns, l_blocks, preferred_element_type=jnp.float32)
    arrived = (columns, pre_act) + tuple(parts[1:])
    columns = arrived[0]
    pre_act = arrived[1]
    pre_rows = lax.all_to_all(pre_act, "feat", split_axis=0, concat_axis=1, tiled=True)
    slope_rows = slope_of(pre_rows, g_blocks)
    slope_cols = lax.all_to_all(slope_rows, "feat", split_axis=1, concat_axis=0, tiled=True)
    back_cols = jnp.einsum(
        "cst,sbc->bst", slope_cols, l_blocks, preferred_element_type=jnp.float32
    ).astype(jnp.bfloat16)
    l_term = jnp.einsum("bst,cst->sbc", columns, slope_cols, preferred_element_type=jnp.float32)
    l_term = l_term.reshape(local_cols, BLOCKS * BLOCKS) * grad_scale
    back_rows = lax.all_to_all(back_cols, "feat", split_axis=0, concat_axis=1, tiled=True)
    back_rows, through_r = (
        back_rows,
        jnp.einsum("bot,bio->bit", back_rows, r_whole, preferred_element_type=jnp.float32),
    )
    grad_x = (
        (g_blocks.astype(jnp.float32) + through_r)
        .astype(jnp.bfloat16)
        .reshape(local_blocks * WIDTH, tok_count)
    )
    r_term = (
        jnp.einsum("bit,bot->bio", x_blocks, back_rows, preferred_element_type=jnp.float32)
        * grad_scale
    )
    grad_l, grad_r = (
        lax.psum_scatter(l_term, "dp", scatter_dimension=1, tiled=True),
        lax.psum_scatter(r_term, "dp", scatter_dimension=1, tiled=True),
    )
    return (grad_x, grad_r, grad_l)


def solution(mesh):
    placed = (P("feat", "dp"), P("feat", "dp"), P("feat", "dp", None), P("feat", "dp"))
    return jax.shard_map(
        body,
        mesh=mesh,
        in_specs=placed,
        out_specs=(P("feat", "dp"), P("feat", "dp", None), P("feat", "dp")),
        check_vma=False,
    )
```

profile of v0, /device:TPU:0, one launch (start us, length us, event | category | flops | bytes accessed | tf_op | source)
XLA Modules:
  0.0 399.9 jit_solution(9625601833998472881)
XLA Ops:
  7.2 0.0 copy-start
  7.2 0.0 all-gather.2.cloned.1.call-start
  7.2 0.7 all-gather.2.cloned.1.call-update
  7.9 54.3 %all-gather.2.cloned.1.call-done = bf16[16,256,256]{2,1,0:T(8,128)(2,1)} async-done(((bf16[16,32,256]{2,1,0:T(8,128)(2,1)}), bf16[16,256,256]{2,1,0:T(8,128)(2,1)}) %all-gather.2.cloned.1.call-update) | async-done | bytes 2097168 | tf_op jit(solution)/shard_map/all_gather | solution.py:25
  62.2 0.0 copy-done
  62.2 2.4 convolution_convert_fusion
  64.6 2.5 copy.19
  67.1 0.0 copy-start.5
  67.1 4.6 %all-to-all-start = ((bf16[16,256,256]{2,0,1:T(8,128)(2,1)}), bf16[16,256,256]{2,0,1:T(8,128)(2,1)}, u32[]{:S(2)}, u32[]{:S(2)}) async-start(bf16[16,256,256]{2,0,1:T(8,128)(2,1)} %copy.19), calls=%async_computation | async-start | bytes 4194304 | tf_op jit(solution)/shard_map/all_to_all | solution.py:36
  71.6 0.0 reduce-scatter.3.cloned.1.call-start
  71.7 0.0 copy-done.5
  71.7 33.3 %all_gather.7 = bf16[64,4096]{1,0:T(8,128)(2,1)} all-gather(bf16[64,512]{1,0:T(8,128)(2,1)S(1)} %copy-done.5), channel_id=1, replica_groups=mesh['dp'=8,'feat'=4] {'dp'}, dimensions={1}, use_global_device_ids=true | all-gather | bytes 589824 | tf_op jit(solution)/shard_map/all_gather | solution.py:26
  105.0 2.1 reshape.22
  107.1 0.0 all-to-all-done
  107.1 1.8 copy.20
  109.0 0.0 copy-start.1
  109.0 1.3 copy-done.1
  110.3 0.8 convolution_bitcast_fusion
  111.0 2.4 copy.22
  113.5 51.1 %all_to_all.72 = f32[64,64,256]{2,1,0:T(8,128)S(1)} all-to-all(f32[64,64,256]{2,1,0:T(8,128)S(1)} %copy.22), channel_id=1, replica_groups=mesh['dp'=8,'feat'=4] {'feat'}, dimensions={0} | all-to-all | bytes 8388608 | tf_op jit(solution)/shard_map/all_to_all | solution.py:42
  164.6 0.0 copy-start.4
  164.6 0.5 copy.23
  165.0 1.1 copy-done.4
  166.1 3.3 fusion.6
  169.5 1.2 copy.24
  170.6 28.2 %all_to_all.73 = bf16[16,256,256]{2,0,1:T(8,128)(2,1)S(1)} all-to-all(bf16[16,256,256]{2,0,1:T(8,128)(2,1)S(1)} %copy.24), channel_id=1, replica_groups=mesh['dp'=8,'feat'=4] {'feat'}, dimensions={1} | all-to-all | bytes 4194304 | tf_op jit(solution)/shard_map/all_to_all | solution.py:44
  198.8 0.3 copy.25
  199.1 0.0 copy-start.2
  199.1 0.7 convert_bitcast_fusion
  199.8 0.6 copy-done.2
  200.4 1.2 copy.26
  201.6 28.2 %all_to_all.74 = bf16[64,64,256]{2,1,0:T(8,128)(2,1)S(1)} all-to-all(bf16[64,64,256]{2,1,0:T(8,128)(2,1)S(1)} %copy.26), channel_id=1, replica_groups=mesh['dp'=8,'feat'=4] {'feat'}, dimensions={0} | all-to-all | bytes 4194304 | tf_op jit(solution)/shard_map/all_to_all | solution.py:50
  229.8 0.2 copy.27
  230.0 0.0 copy-start.3
  230.0 1.3 copy-done.3
  231.4 2.7 multiply_bitcast_fusion
  234.1 5.5 %copy.28 = f32[16,256,256]{2,0,1:T(8,128)} copy(f32[16,256,256]{1,2,0:T(8,128)} %multiply_bitcast_fusion) | data formatting | bytes 8388608 | tf_op jit(solution)/shard_map/mul | solution.py:61
  239.6 0.0 reduce-scatter.3.cloned.1.call-update
  239.6 0.0 reduce-scatter.5.cloned.1.call-start
  239.6 4.2 %convolution_multiply_fusion = f32[64,64,64]{2,1,0:T(8,128)} fusion(bf16[64,64,256]{2,0,1:T(8,128)(2,1)} %bitcast.50, bf16[64,64,256]{2,0,1:T(8,128)(2,1)} %bitcast.52), kind=kOutput, calls=%fused_computation.20 | convolution fusion | flops 134479872 | bytes 5242880 | tf_op jit(solution)/shard_map/bst,cst->sbc/dot_general | solution.py:48
  243.9 3.1 mul.78
  247.0 0.0 reduce-scatter.5.cloned.1.call-update
  247.0 4.9 %fusion.10 = bf16[16,256,256]{2,1,0:T(8,128)(2,1)} fusion(bf16[16,256,256]{2,1,0:T(8,128)(2,1)} %bitcast.58, bf16[16,256,256]{2,1,0:T(8,128)(2,1)} %all-gather.2.cloned.1.call-done, bf16[16,256,256]{2,1,0:T(8,128)(2,1)} %bitcast.54), kind=kOutput, calls=%fused_computation.15 | convolution fusion | flops 540016640 | bytes 8388608 | tf_op jit(solution)/shard_map/bot,bio->bit/dot_general | solution.py:53
  251.9 73.5 %reduce-scatter.3.cloned.1.call-done = f32[16,32,256]{2,0,1:T(8,128)} async-done(((f32[16,256,256]{2,0,1:T(8,128)}), f32[16,32,256]{2,0,1:T(8,128)}) %reduce-scatter.3.cloned.1.call-update) | async-done | bytes 524304 | tf_op jit(solution)/shard_map/reduce_scatter | solution.py:66
  325.4 2.1 copy.29
  327.6 65.8 %reduce-scatter.5.cloned.1.call-done = f32[64,512]{1,0:T(8,128)} async-done(((f32[64,4096]{1,0:T(8,128)}), f32[64,512]{1,0:T(8,128)}) %reduce-scatter.5.cloned.1.call-update) | async-done | bytes 131088 | tf_op jit(solution)/shard_map/reduce_scatter | solution.py:65
Async XLA Ops:
  7.2 55.0 %copy-start = (bf16[4096,256]{1,0:T(8,128)(2,1)S(1)}, bf16[4096,256]{1,0:T(8,128)(2,1)}, u32[]{:S(2)}) copy-start(bf16[4096,256]{1,0:T(8,128)(2,1)} %param.4) | copy-start | bytes 6291460
  7.2 55.0 %all-gather.2.cloned.1.call-start = ((), (), s32[]{:S(2)}) async-start(), calls=%async_computation.6 | async-start | bytes 2359296 | tf_op jit(solution)/shard_map/all_gather | solution.py:25
  67.1 4.6 %copy-start.5 = (bf16[64,512]{1,0:T(8,128)(2,1)S(1)}, bf16[64,512]{1,0:T(8,128)(2,1)}, u32[]{:S(2)}) copy-start(bf16[64,512]{1,0:T(8,128)(2,1)} %param.7) | copy-start | bytes 196612
  67.1 40.0 %all-to-all-start = ((bf16[16,256,256]{2,0,1:T(8,128)(2,1)}), bf16[16,256,256]{2,0,1:T(8,128)(2,1)}, u32[]{:S(2)}, u32[]{:S(2)}) async-start(bf16[16,256,256]{2,0,1:T(8,128)(2,1)} %copy.19), calls=%async_computation | async-start | bytes 4194304 | tf_op jit(solution)/shard_map/all_to_all | solution.py:36
  71.6 253.8 %reduce-scatter.3.cloned.1.call-start = ((), (), s32[]{:S(2)}) async-start(), calls=%async_computation.7 | async-start | bytes 4718592 | tf_op jit(solution)/shard_map/reduce_scatter | solution.py:66
  109.0 1.3 copy-start.1
  164.6 1.6 copy-start.4
  199.1 1.3 copy-start.2
  230.0 1.3 copy-start.3
  239.6 153.8 %reduce-scatter.5.cloned.1.call-start = ((), (), s32[]{:S(2)}) async-start(), calls=%async_computation.8 | async-start | bytes 1179648 | tf_op jit(solution)/shard_map/reduce_scatter | solution.py:65
Sparse Core Ops, SparseCore 0:
  10.2 51.9 all-gather.1
  239.7 85.6 reduce-scatter.2
  329.8 63.5 reduce-scatter.4
where the time goes:
time: 401 us; the launch traced here: 400 us
  waiting for transfers between devices  194 us (48%)
  blocking collectives  141 us (35%)
  local copies, waits for them, and re-layouts  27.3 us (7%)
  matrix products  15.7 us (4%)
  between operations  13.9 us (3%)
  starting transfers between devices  4.69 us (1%)
    reduce_scatter x1, waiting for transfers between devices, body(): lax.psum_scatter(r_term, 'dp', scatter_dimension=1, tiled=True)  73.5 us
    reduce_scatter x1, waiting for transfers between devices, body(): lax.psum_scatter(l_term, 'dp', scatter_dimension=1, tiled=True)  65.8 us
    all_gather x1, waiting for transfers between devices, body(): lax.all_gather(r_mix, 'dp', axis=1, tiled=True)  54.3 us
    all_to_all x1, blocking collectives, body(): lax.all_to_all(pre_act, 'feat', split_axis=0, concat_axis=1, tiled=True)  51.1 us
    all_gather x1, blocking collectives, body(): lax.all_gather(l_mix, 'dp', axis=1, tiled=True)  33.3 us
    all_to_all x1, blocking collectives, body(): lax.all_to_all(slope_rows, 'feat', split_axis=1, concat_axis=0, tiled=True)  28.2 us
    all_to_all x1, blocking collectives, body(): lax.all_to_all(back_cols, 'feat', split_axis=0, concat_axis=1, tiled=True)  28.2 us
  transfers between devices with their start and end apart: 4, of which 3 were waited for; matrix products, arithmetic and copies ran while one was open for 4% of the time, Pallas kernels for 0%

commit v1 on v0

--- a/solution.py
+++ b/solution.py
@@ -6,6 +6,28 @@
 
 BLOCKS = 64
 WIDTH = 256
+
+
+def joined_along(blocks, dim):
+    blocks = jnp.moveaxis(blocks, 0, dim)
+    shape = blocks.shape
+    return blocks.reshape(*shape[:dim], shape[dim] * shape[dim + 1], *shape[dim + 2 :])
+
+
+def ring_gather(value, axis, dim):
+    size = lax.axis_size(axis)
+    pairs = [(i, (i + 1) % size) for i in range(size)]
+    back = [(b, a) for a, b in pairs]
+    lower, upper = ([], [])
+    for hop in range(size - 1):
+        if hop % 2 == 0:
+            lower.append(lax.ppermute(lower[-1] if lower else value, axis, pairs))
+        else:
+            upper.append(lax.ppermute(upper[-1] if upper else value, axis, back))
+    pieces = jnp.stack([*lower[::-1], value, *upper])
+    shift = lax.axis_index(axis) - len(lower)
+    pieces = pieces[(jnp.arange(size) - shift) % size]
+    return joined_along(pieces, dim)
 
 
 def gelu_tanh(values):
@@ -23,7 +45,7 @@
     grad_scale = 1.0 / math.sqrt(tok_count * lax.axis_size("dp"))
     r_whole, l_whole = (
         lax.all_gather(r_mix, "dp", axis=1, tiled=True),
-        lax.all_gather(l_mix, "dp", axis=1, tiled=True),
+        ring_gather(l_mix, "dp", 1),
     )
     local_cols = l_whole.shape[0]
     l_blocks = l_whole.reshape(local_cols, BLOCKS, BLOCKS)

time: 401 us -> 392 us (0.978)
  blocking collectives: 141 us -> 107 us
  starting transfers between devices: 4.69 us -> 22.7 us
  waiting for transfers between devices: 194 us -> 200 us
    all_gather x1 -> x0, blocking collectives: 33.3 us -> none  [body(): lax.all_gather(l_mix, 'dp', axis=1, tiled=True)]
    all_gather x1, waiting for transfers between devices: 54.3 us -> 25.5 us  [body(): lax.all_gather(r_mix, 'dp', axis=1, tiled=True)]
    all_to_all x1, waiting for transfers between devices: 0.01 us -> 22.3 us  [body(): lax.all_to_all(outgoing[0], 'feat', split_axis=1, concat_axis=0, tiled=True)]
    ppermute x0 -> x7, starting transfers between devices: none -> 18 us  [the longest x3 15 us: ring_gather(): upper.append(lax.ppermute(upper[-1] if upper else value, axis, back))]
    ppermute x0 -> x7, waiting for transfers between devices: none -> 12.7 us  [the longest x4 11.8 us: ring_gather(): lower.append(lax.ppermute(lower[-1] if lower else value, axis, pairs))]
  transfers between devices with their start and end apart: 4 -> 11, of which waited for: 3 -> 9; matrix products, arithmetic and copies ran while one was open for 4% -> 6% of each run, Pallas kernels for 0% -> 0%
where the time goes in v1:
time: 392 us
  waiting for transfers between devices  200 us (51%)
  blocking collectives  107 us (27%)
  local copies, waits for them, and re-layouts  28.6 us (7%)
  starting transfers between devices  22.7 us (6%)
  matrix products  15.8 us (4%)
  between operations  14 us (4%)
    reduce_scatter x1, waiting for transfers between devices, body(): lax.psum_scatter(r_term, 'dp', scatter_dimension=1, tiled=True)  73.3 us
    reduce_scatter x1, waiting for transfers between devices, body(): lax.psum_scatter(l_term, 'dp', scatter_dimension=1, tiled=True)  65.8 us
    all_to_all x1, blocking collectives, body(): lax.all_to_all(pre_act, 'feat', split_axis=0, concat_axis=1, tiled=True)  50.7 us
    all_to_all x1, blocking collectives, body(): lax.all_to_all(slope_rows, 'feat', split_axis=1, concat_axis=0, tiled=True)  28.2 us
    all_to_all x1, blocking collectives, body(): lax.all_to_all(back_cols, 'feat', split_axis=0, concat_axis=1, tiled=True)  28.2 us
    all_gather x1, waiting for transfers between devices, body(): lax.all_gather(r_mix, 'dp', axis=1, tiled=True)  25.5 us
    all_to_all x1, waiting for transfers between devices, body(): lax.all_to_all(outgoing[0], 'feat', split_axis=1, concat_axis=0, tiled=True)  22.3 us
    ppermute x3, starting transfers between devices, ring_gather(): upper.append(lax.ppermute(upper[-1] if upper else value, axis, back))  15 us
  transfers between devices with their start and end apart: 11, of which 9 were waited for; matrix products, arithmetic and copies ran while one was open for 6% of the time, Pallas kernels for 0%

profile of v1, /device:TPU:0, one launch (start us, length us, event | category | flops | bytes accessed | tf_op | source)
XLA Modules:
  0.0 391.7 jit_solution(11947656834468680656)
XLA Ops:
  7.2 0.0 copy-start
  7.2 0.0 all-gather.2.cloned.1.call-start
  7.2 0.7 all-gather.2.cloned.1.call-update
  7.9 3.0 collective-permute-start
  10.9 5.5 %collective-permute-done = bf16[64,512]{1,0:T(8,128)(2,1)S(1)} collective-permute-done((bf16[64,512]{1,0:T(8,128)(2,1)}, bf16[64,512]{1,0:T(8,128)(2,1)S(1)}, u32[]{:S(2)}, u32[]{:S(2)}) %collective-permute-start) | collective-permute-done | bytes 65568 | tf_op jit(solution)/shard_map/ppermute | solution.py:24
  16.4 0.0 collective-permute-start.1
  16.4 4.7 %collective-permute-start.4 = (bf16[64,512]{1,0:T(8,128)(2,1)}, bf16[64,512]{1,0:T(8,128)(2,1)S(1)}, u32[]{:S(2)}, u32[]{:S(2)}) collective-permute-start(bf16[64,512]{1,0:T(8,128)(2,1)} %param.7), channel_id=1, source_target_pairs={{4,0},{8,4},{12,8},{16,12},{20,16},{24,20},{28,24},{0,28},{5,1},{9... | collective-permute-start | bytes 196616 | tf_op jit(solution)/shard_map/ppermute | solution.py:26
  21.2 2.2 collective-permute-done.1
  23.4 0.0 collective-permute-start.2
  23.4 0.9 collective-permute-done.4
  24.3 5.1 %collective-permute-start.5 = (bf16[64,512]{1,0:T(8,128)(2,1)S(1)}, bf16[64,512]{1,0:T(8,128)(2,1)S(1)}, u32[]{:S(2)}, u32[]{:S(2)}) collective-permute-start(bf16[64,512]{1,0:T(8,128)(2,1)S(1)} %collective-permute-done.4), channel_id=1, source_target_pairs={{4,0},{8,4},{12,8},{16,12},{20,16},{24,20},{28,24},{0,28},{5,1},{9... | collective-permute-start | bytes 196616 | tf_op jit(solution)/shard_map/ppermute | solution.py:26
  29.5 2.3 collective-permute-done.2
  31.7 0.0 collective-permute-start.3
  31.7 0.0 collective-permute-done.5
  31.7 5.2 %collective-permute-start.6 = (bf16[64,512]{1,0:T(8,128)(2,1)S(1)}, bf16[64,512]{1,0:T(8,128)(2,1)S(1)}, u32[]{:S(2)}, u32[]{:S(2)}) collective-permute-start(bf16[64,512]{1,0:T(8,128)(2,1)S(1)} %collective-permute-done.5), channel_id=1, source_target_pairs={{4,0},{8,4},{12,8},{16,12},{20,16},{24,20},{28,24},{0,28},{5,1},{9... | collective-permute-start | bytes 196616 | tf_op jit(solution)/shard_map/ppermute | solution.py:26
  36.9 1.8 collective-permute-done.3
  38.7 25.5 %all-gather.2.cloned.1.call-done = bf16[16,256,256]{2,1,0:T(8,128)(2,1)} async-done(((bf16[16,32,256]{2,1,0:T(8,128)(2,1)}), bf16[16,256,256]{2,1,0:T(8,128)(2,1)}) %all-gather.2.cloned.1.call-update) | async-done | bytes 2097168 | tf_op jit(solution)/shard_map/all_gather | solution.py:47
  64.2 0.0 copy-done
  64.2 2.4 convolution_convert_fusion
  66.5 2.5 copy.21
  69.0 0.0 copy-start.5
  69.0 4.6 %all-to-all-start = ((bf16[16,256,256]{2,0,1:T(8,128)(2,1)}), bf16[16,256,256]{2,0,1:T(8,128)(2,1)}, u32[]{:S(2)}, u32[]{:S(2)}) async-start(bf16[16,256,256]{2,0,1:T(8,128)(2,1)} %copy.21), calls=%async_computation | async-start | bytes 4194304 | tf_op jit(solution)/shard_map/all_to_all | solution.py:58
  73.6 0.0 reduce-scatter.3.cloned.1.call-start
  73.7 0.0 copy-done.5
  73.8 0.0 collective-permute-done.6
  73.8 0.6 gather_fusion
  74.4 1.1 copy.20
  75.5 1.6 reshape_reshape.3
  77.1 22.3 %all-to-all-done = bf16[16,256,256]{2,0,1:T(8,128)(2,1)} async-done(((bf16[16,256,256]{2,0,1:T(8,128)(2,1)}), bf16[16,256,256]{2,0,1:T(8,128)(2,1)}, u32[]{:S(2)}, u32[]{:S(2)}) %all-to-all-start) | async-done | bytes 2097184 | tf_op jit(solution)/shard_map/all_to_all | solution.py:58
  99.4 1.9 copy.22
  101.3 0.0 copy-start.1
  101.3 1.3 copy-done.1
  102.6 0.8 convolution_bitcast_fusion
  103.4 2.4 copy.24
  105.8 50.7 %all_to_all.72 = f32[64,64,256]{2,1,0:T(8,128)S(1)} all-to-all(f32[64,64,256]{2,1,0:T(8,128)S(1)} %copy.24), channel_id=1, replica_groups=mesh['dp'=8,'feat'=4] {'feat'}, dimensions={0} | all-to-all | bytes 8388608 | tf_op jit(solution)/shard_map/all_to_all | solution.py:64
  156.5 0.0 copy-start.4
  156.5 0.5 copy.25
  157.0 1.1 copy-done.4
  158.1 3.3 fusion.6
  161.4 1.2 copy.26
  162.6 28.2 %all_to_all.73 = bf16[16,256,256]{2,0,1:T(8,128)(2,1)S(1)} all-to-all(bf16[16,256,256]{2,0,1:T(8,128)(2,1)S(1)} %copy.26), channel_id=1, replica_groups=mesh['dp'=8,'feat'=4] {'feat'}, dimensions={1} | all-to-all | bytes 4194304 | tf_op jit(solution)/shard_map/all_to_all | solution.py:66
  190.8 0.3 copy.27
  191.1 0.0 copy-start.2
  191.1 0.7 convert_bitcast_fusion
  191.8 0.6 copy-done.2
  192.4 1.2 copy.28
  193.6 28.2 %all_to_all.74 = bf16[64,64,256]{2,1,0:T(8,128)(2,1)S(1)} all-to-all(bf16[64,64,256]{2,1,0:T(8,128)(2,1)S(1)} %copy.28), channel_id=1, replica_groups=mesh['dp'=8,'feat'=4] {'feat'}, dimensions={0} | all-to-all | bytes 4194304 | tf_op jit(solution)/shard_map/all_to_all | solution.py:72
  221.8 0.2 copy.29
  222.0 0.0 copy-start.3
  222.0 1.3 copy-done.3
  223.4 2.8 multiply_bitcast_fusion
  226.1 5.5 %copy.30 = f32[16,256,256]{2,0,1:T(8,128)} copy(f32[16,256,256]{1,2,0:T(8,128)} %multiply_bitcast_fusion) | data formatting | bytes 8388608 | tf_op jit(solution)/shard_map/mul | solution.py:83
  231.6 0.0 reduce-scatter.3.cloned.1.call-update
  231.6 0.0 reduce-scatter.5.cloned.1.call-start
  231.7 4.3 %convolution_multiply_fusion = f32[64,64,64]{2,1,0:T(8,128)} fusion(bf16[64,64,256]{2,0,1:T(8,128)(2,1)} %bitcast.69, bf16[64,64,256]{2,0,1:T(8,128)(2,1)} %bitcast.71), kind=kOutput, calls=%fused_computation.21 | convolution fusion | flops 134479872 | bytes 5242880 | tf_op jit(solution)/shard_map/bst,cst->sbc/dot_general | solution.py:70
  235.9 3.0 mul.78
  239.0 0.0 reduce-scatter.5.cloned.1.call-update
  239.0 4.9 %fusion.10 = bf16[16,256,256]{2,1,0:T(8,128)(2,1)} fusion(bf16[16,256,256]{2,1,0:T(8,128)(2,1)} %bitcast.77, bf16[16,256,256]{2,1,0:T(8,128)(2,1)} %all-gather.2.cloned.1.call-done, bf16[16,256,256]{2,1,0:T(8,128)(2,1)} %bitcast.73), kind=kOutput, calls=%fused_computation.16 | convolution fusion | flops 540016640 | bytes 8388608 | tf_op jit(solution)/shard_map/bot,bio->bit/dot_general | solution.py:75
  243.9 73.3 %reduce-scatter.3.cloned.1.call-done = f32[16,32,256]{2,0,1:T(8,128)} async-done(((f32[16,256,256]{2,0,1:T(8,128)}), f32[16,32,256]{2,0,1:T(8,128)}) %reduce-scatter.3.cloned.1.call-update) | async-done | bytes 524304 | tf_op jit(solution)/shard_map/reduce_scatter | solution.py:88
  317.2 2.1 copy.31
  319.4 65.8 %reduce-scatter.5.cloned.1.call-done = f32[64,512]{1,0:T(8,128)} async-done(((f32[64,4096]{1,0:T(8,128)}), f32[64,512]{1,0:T(8,128)}) %reduce-scatter.5.cloned.1.call-update) | async-done | bytes 131088 | tf_op jit(solution)/shard_map/reduce_scatter | solution.py:87
  (10 shorter events, 0.1 us)
Async XLA Ops:
  7.2 57.0 %copy-start = (bf16[4096,256]{1,0:T(8,128)(2,1)S(1)}, bf16[4096,256]{1,0:T(8,128)(2,1)}, u32[]{:S(2)}) copy-start(bf16[4096,256]{1,0:T(8,128)(2,1)} %param.4) | copy-start | bytes 6291460
  7.2 57.0 %all-gather.2.cloned.1.call-start = ((), (), s32[]{:S(2)}) async-start(), calls=%async_computation.6 | async-start | bytes 2359296 | tf_op jit(solution)/shard_map/all_gather | solution.py:47
  7.9 8.5 %collective-permute-start = (bf16[64,512]{1,0:T(8,128)(2,1)}, bf16[64,512]{1,0:T(8,128)(2,1)S(1)}, u32[]{:S(2)}, u32[]{:S(2)}) collective-permute-start(bf16[64,512]{1,0:T(8,128)(2,1)} %param.7), channel_id=1, source_target_pairs={{0,4},{4,8},{8,12},{12,16},{16,20},{20,24},{24,28},{28,0},{1,5},{5... | collective-permute-start | bytes 196616 | tf_op jit(solution)/shard_map/ppermute | solution.py:24
  16.4 7.0 %collective-permute-start.1 = (bf16[64,512]{1,0:T(8,128)(2,1)S(1)}, bf16[64,512]{1,0:T(8,128)(2,1)S(1)}, u32[]{:S(2)}, u32[]{:S(2)}) collective-permute-start(bf16[64,512]{1,0:T(8,128)(2,1)S(1)} %collective-permute-done), channel_id=1, source_target_pairs={{0,4},{4,8},{8,12},{12,16},{16,20},{20,24},{24,28},{28,0},{1,5},{5... | collective-permute-start | bytes 196616 | tf_op jit(solution)/shard_map/ppermute | solution.py:24
  16.4 7.9 %collective-permute-start.4 = (bf16[64,512]{1,0:T(8,128)(2,1)}, bf16[64,512]{1,0:T(8,128)(2,1)S(1)}, u32[]{:S(2)}, u32[]{:S(2)}) collective-permute-start(bf16[64,512]{1,0:T(8,128)(2,1)} %param.7), channel_id=1, source_target_pairs={{4,0},{8,4},{12,8},{16,12},{20,16},{24,20},{28,24},{0,28},{5,1},{9... | collective-permute-start | bytes 196616 | tf_op jit(solution)/shard_map/ppermute | solution.py:26
  23.4 8.3 %collective-permute-start.2 = (bf16[64,512]{1,0:T(8,128)(2,1)S(1)}, bf16[64,512]{1,0:T(8,128)(2,1)S(1)}, u32[]{:S(2)}, u32[]{:S(2)}) collective-permute-start(bf16[64,512]{1,0:T(8,128)(2,1)S(1)} %collective-permute-done.1), channel_id=1, source_target_pairs={{0,4},{4,8},{8,12},{12,16},{16,20},{20,24},{24,28},{28,0},{1,5},{5... | collective-permute-start | bytes 196616 | tf_op jit(solution)/shard_map/ppermute | solution.py:24
  24.3 7.4 %collective-permute-start.5 = (bf16[64,512]{1,0:T(8,128)(2,1)S(1)}, bf16[64,512]{1,0:T(8,128)(2,1)S(1)}, u32[]{:S(2)}, u32[]{:S(2)}) collective-permute-start(bf16[64,512]{1,0:T(8,128)(2,1)S(1)} %collective-permute-done.4), channel_id=1, source_target_pairs={{4,0},{8,4},{12,8},{16,12},{20,16},{24,20},{28,24},{0,28},{5,1},{9... | collective-permute-start | bytes 196616 | tf_op jit(solution)/shard_map/ppermute | solution.py:26
  31.7 7.0 %collective-permute-start.3 = (bf16[64,512]{1,0:T(8,128)(2,1)S(1)}, bf16[64,512]{1,0:T(8,128)(2,1)S(1)}, u32[]{:S(2)}, u32[]{:S(2)}) collective-permute-start(bf16[64,512]{1,0:T(8,128)(2,1)S(1)} %collective-permute-done.2), channel_id=1, source_target_pairs={{0,4},{4,8},{8,12},{12,16},{16,20},{20,24},{24,28},{28,0},{1,5},{5... | collective-permute-start | bytes 196616 | tf_op jit(solution)/shard_map/ppermute | solution.py:24
  31.7 42.0 %collective-permute-start.6 = (bf16[64,512]{1,0:T(8,128)(2,1)S(1)}, bf16[64,512]{1,0:T(8,128)(2,1)S(1)}, u32[]{:S(2)}, u32[]{:S(2)}) collective-permute-start(bf16[64,512]{1,0:T(8,128)(2,1)S(1)} %collective-permute-done.5), channel_id=1, source_target_pairs={{4,0},{8,4},{12,8},{16,12},{20,16},{24,20},{28,24},{0,28},{5,1},{9... | collective-permute-start | bytes 196616 | tf_op jit(solution)/shard_map/ppermute | solution.py:26
  69.0 4.7 %copy-start.5 = (bf16[64,512]{1,0:T(8,128)(2,1)S(1)}, bf16[64,512]{1,0:T(8,128)(2,1)}, u32[]{:S(2)}) copy-start(bf16[64,512]{1,0:T(8,128)(2,1)} %param.7) | copy-start | bytes 196612
  69.0 30.4 %all-to-all-start = ((bf16[16,256,256]{2,0,1:T(8,128)(2,1)}), bf16[16,256,256]{2,0,1:T(8,128)(2,1)}, u32[]{:S(2)}, u32[]{:S(2)}) async-start(bf16[16,256,256]{2,0,1:T(8,128)(2,1)} %copy.21), calls=%async_computation | async-start | bytes 4194304 | tf_op jit(solution)/shard_map/all_to_all | solution.py:58
  73.6 243.6 %reduce-scatter.3.cloned.1.call-start = ((), (), s32[]{:S(2)}) async-start(), calls=%async_computation.7 | async-start | bytes 4718592 | tf_op jit(solution)/shard_map/reduce_scatter | solution.py:88
  101.3 1.3 copy-start.1
  156.5 1.6 copy-start.4
  191.1 1.4 copy-start.2
  222.0 1.3 copy-start.3
  231.6 153.6 %reduce-scatter.5.cloned.1.call-start = ((), (), s32[]{:S(2)}) async-start(), calls=%async_computation.8 | async-start | bytes 1179648 | tf_op jit(solution)/shard_map/reduce_scatter | solution.py:87
Sparse Core Ops, SparseCore 0:
  10.2 53.9 all-gather.1
  231.7 85.4 reduce-scatter.2
  321.6 63.5 reduce-scatter.4
